TPU v7x, 256 devices: a whole 4x4x8 slice. The times are simulated.
256 devices in a mesh: seq: 32 (over x, z), head: 8 (over y, core).
Axes of the slice: x: 4, y: 4, z: 8, core: 2. Of those that a mesh axis runs over, the one named last changes fastest.
Arguments:
- queries: bfloat16 [4, 8192, 2048], P(None, 'seq', 'head'), may hold values from -6 to 6
- keys: bfloat16 [4, 8192, 2048], P(None, 'seq', 'head'), may hold values from -6 to 6
- values: bfloat16 [4, 8192, 2048], P(None, 'seq', 'head'), may hold values from -6 to 6
- out_grad: bfloat16 [4, 8192, 2048], P(None, ('seq', 'head')), may hold values from -6 to 6
- selected: int32 [4, 32, 16, 2], P(None, None, 'head'), may hold values from 0 to 63, as said below
Outputs:
- attended: bfloat16 [4, 8192, 2048], P(None, 'seq', 'head')
- query_gradient: bfloat16 [4, 8192, 2048], P(None, 'seq', 'head')
- key_grad: bfloat16 [4, 8192, 2048], P(None, 'seq', 'head')
- value_grad: bfloat16 [4, 8192, 2048], P(None, 'seq', 'head')
Inputs may be any that keep to these rules, and one draw needn't show every extreme that they name: selected[f, s, h, j] selects for head h an earlier block of the query block that device s holds in slice f (block s // 2, 31 - s // 2, 32 + s // 2, 63 - s // 2 for f = 0, 1, 2, 3); an entry not smaller than that block's number selects nothing. Rows 2 m and 2 m + 1 are equal. Let the group of block b be r or 31 - r, whichever is smaller, with r = b mod 32. For one head and one m, the usable entries of the four query blocks lie in different groups, none of them group m.
All inputs are finite; a program needn't handle non-finite values.
Results may differ from a plain program's by a relative error of at most 0.0074.
Values may be sent and summed in bfloat16 or wider, within the bound.
No kernel may reach another device: no remote copies, remote signals or barrier semaphores. Data moves between devices by JAX's collectives and lax.ppermute only.
A program may use at most 128 MiB of HBM per device.

v0:
```python
import math

import jax
import jax.numpy as jnp
from jax import lax
from jax.sharding import PartitionSpec as P

HD = 128


def from_partner(value, axis, bit):
    return lax.ppermute(value, axis, [(i, i ^ 1 << bit) for i in range(lax.axis_size(axis))])


def per_head(stored, head_count):
    slices = stored.shape[0]
    rows = stored.shape[1]
    return stored.reshape(slices, rows, head_count, HD).transpose(2, 0, 1, 3)


def merge_heads(split):
    head_count = split.shape[0]
    slices = split.shape[1]
    rows = split.shape[2]
    return split.transpose(1, 2, 0, 3).reshape(slices, rows, head_count * HD)


def span_owner(block, half_bit, seq_count):
    fold = block % seq_count
    flip = (fold >= seq_count // 2).astype(jnp.int32)
    pair_id = jnp.where(flip == 1, seq_count - 1 - fold, fold)
    return 2 * pair_id + (half_bit + flip) % 2


def pick_blocks(received, owner_ids):
    count = received.shape[1]
    half_len = received.shape[2]
    slices = owner_ids.shape[0]
    width = owner_ids.shape[2] * 2 * half_len
    head_index = jnp.arange(count, dtype=jnp.int32)[None, :, None, None]
    taken = received[owner_ids, head_index]
    taken = taken.transpose(1, 0, 2, 3, 4, 5)
    return taken.reshape(count, slices, width, HD)


def local(queries, keys, values, out_grad, selected):
    seq_count = lax.axis_size("seq")
    my_index = lax.axis_index("seq")
    parity = my_index % 2
    group_id = my_index // 2
    slices = queries.shape[0]
    half_len = queries.shape[1]
    block_len = 2 * half_len
    head_count = queries.shape[2] // HD
    logit_scale_factor = 1.0 / math.sqrt(HD)
    q_heads = per_head(queries, head_count)
    k_heads = per_head(keys, head_count)
    v_heads = per_head(values, head_count)
    grad_rows = lax.all_to_all(out_grad, "head", split_axis=2, concat_axis=1, tiled=True)
    g_heads = per_head(grad_rows, head_count)
    sources = jnp.arange(seq_count, dtype=jnp.int32)
    src_group = sources // 2
    query_block = jnp.stack(
        [src_group, seq_count - 1 - src_group, seq_count + src_group, 2 * seq_count - 1 - src_group]
    )
    usable_all = selected < query_block[:, :, None, None]
    mine_block = jnp.stack(
        [group_id, seq_count - 1 - group_id, seq_count + group_id, 2 * seq_count - 1 - group_id]
    )
    hits = usable_all[..., None] & (selected[..., None] == mine_block)
    need = jnp.any(hits, axis=(0, 3)).astype(jnp.float32)
    need_low = need.astype(jnp.bfloat16)
    mine_sel = lax.dynamic_index_in_dim(selected, my_index, 1, keepdims=False)
    mine_usable = mine_sel < mine_block[:, None, None]
    halves = jnp.arange(2, dtype=jnp.int32)
    owner_raw = span_owner(mine_sel[..., None], halves, seq_count)
    owners = jnp.where(mine_usable[..., None], owner_raw, 0)
    held_half = (jnp.arange(slices, dtype=jnp.int32) + parity) % 2
    pairs_k = k_heads.reshape(head_count, slices // 2, 2, half_len, HD)
    pairs_v = v_heads.reshape(head_count, slices // 2, 2, half_len, HD)
    lead_k = jnp.where(parity == 0, pairs_k[:, :, 0], pairs_k[:, :, 1])
    lead_v = jnp.where(parity == 0, pairs_v[:, :, 0], pairs_v[:, :, 1])
    send_k = jnp.einsum(
        "rhf,hfld->rhld", need_low, k_heads, preferred_element_type=jnp.float32
    ).astype(jnp.bfloat16)
    send_v = jnp.einsum(
        "rhf,hfld->rhld", need_low, v_heads, preferred_element_type=jnp.float32
    ).astype(jnp.bfloat16)
    got_k, got_v = (
        lax.all_to_all(send_k, "seq", split_axis=0, concat_axis=0, tiled=True),
        lax.all_to_all(send_v, "seq", split_axis=0, concat_axis=0, tiled=True),
    )
    sel_k = pick_blocks(got_k, owners)
    sel_v = pick_blocks(got_v, owners)
    mate_k, mate_v = from_partner((lead_k, lead_v), "seq", 0)
    empty_span = jnp.zeros((head_count, half_len, HD), jnp.bfloat16)
    own_keys = []
    own_values = []
    for slice_id in range(slices):
        pair_at = slice_id // 2
        second_k = jnp.concatenate([mate_k[:, pair_at], k_heads[:, slice_id]], axis=1)
        first_k = jnp.concatenate([k_heads[:, slice_id], empty_span], axis=1)
        second_v = jnp.concatenate([mate_v[:, pair_at], v_heads[:, slice_id]], axis=1)
        first_v = jnp.concatenate([v_heads[:, slice_id], empty_span], axis=1)
        own_keys.append(jnp.where(held_half[slice_id] == 1, second_k, first_k))
        own_values.append(jnp.where(held_half[slice_id] == 1, second_v, first_v))
    every_key_row = jnp.concatenate([jnp.stack(own_keys, axis=1), sel_k], axis=2)
    every_value_row = jnp.concatenate([jnp.stack(own_values, axis=1), sel_v], axis=2)
    key_pos = jnp.arange(block_len, dtype=jnp.int32)
    query_pos = held_half[:, None] * half_len + jnp.arange(half_len, dtype=jnp.int32)[None, :]
    own_vis = key_pos[None, None, :] <= query_pos[:, :, None]
    sel_vis = jnp.repeat(mine_usable.transpose(1, 0, 2), block_len, axis=2)
    visible = jnp.concatenate(
        [
            jnp.broadcast_to(own_vis[None], (head_count, slices, half_len, block_len)),
            jnp.broadcast_to(
                sel_vis[:, :, None, :], (head_count, slices, half_len, sel_vis.shape[2])
            ),
        ],
        axis=-1,
    )

    def attend(operands):
        q_one, k_one, v_one, g_one, vis_one = operands
        attention_logits = (
            jnp.einsum("hqd,hkd->hqk", q_one, k_one, preferred_element_type=jnp.float32)
            * logit_scale_factor
        )
        masked = jnp.where(vis_one, attention_logits, -jnp.inf)
        row_max = jnp.max(masked, axis=-1, keepdims=True)
        exp_vals = jnp.exp(masked - row_max)
        probs = exp_vals / jnp.sum(exp_vals, axis=-1, keepdims=True)
        probability_narrow = probs.astype(jnp.bfloat16)
        attended = jnp.einsum(
            "hqk,hkd->hqd", probability_narrow, v_one, preferred_element_type=jnp.float32
        ).astype(jnp.bfloat16)
        probability_gradient = jnp.einsum(
            "hqd,hkd->hqk", g_one, v_one, preferred_element_type=jnp.float32
        )
        row_delta = jnp.sum(probs * probability_gradient, axis=-1, keepdims=True)
        score_gradient = (probs * (probability_gradient - row_delta)).astype(jnp.bfloat16)
        query_gradient = (
            logit_scale_factor
            * jnp.einsum("hqk,hkd->hqd", score_gradient, k_one, preferred_element_type=jnp.float32)
        ).astype(jnp.bfloat16)
        key_terms = logit_scale_factor * jnp.einsum(
            "hqk,hqd->hkd", score_gradient, q_one, preferred_element_type=jnp.float32
        )
        value_terms = jnp.einsum(
            "hqk,hqd->hkd", probability_narrow, g_one, preferred_element_type=jnp.float32
        )
        return (attended, query_gradient, key_terms, value_terms)

    def leading_slice(array):
        return jnp.moveaxis(array, 1, 0)

    attended, query_gradient, key_terms, value_terms = lax.map(
        attend,
        (
            leading_slice(q_heads),
            leading_slice(every_key_row),
            leading_slice(every_value_row),
            leading_slice(g_heads),
            leading_slice(visible),
        ),
    )
    sel_dest = jnp.where(mine_usable[..., None], owner_raw, -1)
    item_count = slices * sel_dest.shape[2] * 2
    dest_items = sel_dest.transpose(1, 0, 2, 3).reshape(head_count, item_count)
    routing = (dest_items[None] == sources[:, None, None]).astype(jnp.float32)

    def outgoing(terms):
        items = terms[:, :, block_len:].reshape(
            slices, head_count, item_count // slices, half_len * HD
        )
        items = items.transpose(1, 0, 2, 3).reshape(head_count, item_count, half_len * HD)
        summed = jnp.einsum("shi,hix->shx", routing, items, precision=lax.Precision.HIGHEST)
        return summed.astype(jnp.bfloat16).reshape(seq_count, head_count, half_len, HD)

    def trailing(terms):
        by_pair = terms[:, :, :half_len].reshape(slices // 2, 2, head_count, half_len, HD)
        return jnp.where(parity == 0, by_pair[:, 1], by_pair[:, 0]).astype(jnp.bfloat16)

    back_k, back_v = (
        lax.all_to_all(outgoing(key_terms), "seq", split_axis=0, concat_axis=0, tiled=True),
        lax.all_to_all(outgoing(value_terms), "seq", split_axis=0, concat_axis=0, tiled=True),
    )
    mate_back_k, mate_back_v = from_partner((trailing(key_terms), trailing(value_terms)), "seq", 0)
    gathered_k = jnp.einsum("rhf,rhld->hfld", need_low, back_k, preferred_element_type=jnp.float32)
    gathered_v = jnp.einsum("rhf,rhld->hfld", need_low, back_v, preferred_element_type=jnp.float32)

    def own_part(terms, mate_back):
        rows_kept = []
        for slice_id in range(slices):
            first = terms[slice_id, :, :half_len] + mate_back[slice_id // 2].astype(jnp.float32)
            second = terms[slice_id, :, half_len:block_len]
            rows_kept.append(jnp.where(held_half[slice_id] == 0, first, second))
        return jnp.stack(rows_kept, axis=1)

    key_grad = (own_part(key_terms, mate_back_k) + gathered_k).astype(jnp.bfloat16)
    value_grad = (own_part(value_terms, mate_back_v) + gathered_v).astype(jnp.bfloat16)
    attended_rows = attended.transpose(0, 2, 1, 3).reshape(slices, half_len, head_count * HD)
    query_rows = query_gradient.transpose(0, 2, 1, 3).reshape(slices, half_len, head_count * HD)
    return (attended_rows, query_rows, merge_heads(key_grad), merge_heads(value_grad))


def solution(mesh):
    in_specs = (
        P(None, "seq", "head"),
        P(None, "seq", "head"),
        P(None, "seq", "head"),
        P(None, ("seq", "head"), None),
        P(None, None, "head", None),
    )
    out_specs = (
        P(None, "seq", "head"),
        P(None, "seq", "head"),
        P(None, "seq", "head"),
        P(None, "seq", "head"),
    )
    return jax.shard_map(local, mesh=mesh, in_specs=in_specs, out_specs=out_specs, check_vma=False)
```

profile of v0, /device:TPU:1, one launch (start us, length us, event | category | flops | bytes accessed | tf_op | source)
XLA Modules:
  0.0 598.6 jit_solution(1851862565930724758)
XLA Ops:
  0.7 2.9 copy.156
  6.2 6.6 %all-to-all-start.2 = ((bf16[8,2,16384]{2,1,0:T(2,128)(2,1)}), bf16[8,2,16384]{2,1,0:T(2,128)(2,1)S(1)}, u32[]{:S(2)}, u32[]{:S(2)}) async-start(bf16[8,2,16384]{2,1,0:T(2,128)(2,1)} %reshape.621), calls=%async_computation.2 | async-start | bytes 1048576 | tf_op jit(solution)/shard_map/all_to_all | solution.py:59
  14.9 3.6 copy.144
  18.4 3.7 all-to-all-done.2
  23.0 10.5 %all-to-all-start = ((bf16[32,2,256,128]{3,2,1,0:T(8,128)(2,1)}), bf16[32,2,256,128]{3,2,1,0:T(8,128)(2,1)}, u32[]{:S(2)}, u32[]{:S(2)}) async-start(bf16[32,2,256,128]{3,2,1,0:T(8,128)(2,1)} %copy.144), calls=%async_computation | async-start | bytes 8388608 | tf_op jit(solution)/shard_map/all_to_all | solution.py:90
  35.3 3.5 copy.154
  38.8 87.5 %all-to-all-done = bf16[32,2,256,128]{3,2,1,0:T(8,128)(2,1)} async-done(((bf16[32,2,256,128]{3,2,1,0:T(8,128)(2,1)}), bf16[32,2,256,128]{3,2,1,0:T(8,128)(2,1)}, u32[]{:S(2)}, u32[]{:S(2)}) %all-to-all-start) | async-done | bytes 4194336 | tf_op jit(solution)/shard_map/all_to_all | solution.py:90
  126.3 9.6 %all-to-all-start.1 = ((bf16[32,2,256,128]{3,2,1,0:T(8,128)(2,1)}), bf16[32,2,256,128]{3,2,1,0:T(8,128)(2,1)}, u32[]{:S(2)}, u32[]{:S(2)}) async-start(bf16[32,2,256,128]{3,2,1,0:T(8,128)(2,1)} %copy.154), calls=%async_computation.1 | async-start | bytes 8388608 | tf_op jit(solution)/shard_map/all_to_all | solution.py:91
  141.4 4.3 add_bitcast_fusion
  150.6 87.9 %collective-permute-done.1 = bf16[2,2,256,128]{2,3,0,1:T(8,128)(2,1)S(1)} collective-permute-done((bf16[2,2,256,128]{2,3,0,1:T(8,128)(2,1)S(1)}, bf16[2,2,256,128]{2,3,0,1:T(8,128)(2,1)S(1)}, u32[]{:S(2)}, u32[]{:S(2)}) %collective-permute-start.1) | collective-permute-done | bytes 262176 | tf_op jit(solution)/shard_map/ppermute | solution.py:12
  243.2 3.6 reshape.622
  251.0 3.1 gather_fusion
  254.2 3.1 maximum_bitcast_fusion
  257.3 3.1 gather_fusion.1
  262.3 77.3 %while.16 = (s32[]{:T(128)}, bf16[4,2,256,128]{3,2,1,0:T(8,128)(2,1)}, bf16[4,2,256,128]{3,2,1,0:T(8,128)(2,1)}, f32[4,2,1536,128]{3,2,1,0:T(8,128)}, f32[4,2,15...) while((s32[]{:T(128)}, ...), condition=%wide.region_5.6_spmd, body=%wide.region_1.5_spmd.sunk | while | flops 1627722752 | bytes 32004220 | solution.py:157
  263.5 2.7 fusion.182
  266.2 3.8 fusion.183
  274.7 2.8 fusion.185
  277.5 4.3 fusion.186
  282.8 2.7 fusion.182
  285.5 3.8 fusion.183
  294.0 2.8 fusion.185
  296.7 4.4 fusion.186
  302.1 2.7 fusion.182
  304.8 3.8 fusion.183
  313.3 2.8 fusion.185
  316.1 4.3 fusion.186
  321.4 2.7 fusion.182
  324.0 3.8 fusion.183
  332.5 2.8 fusion.185
  335.4 4.3 fusion.186
  339.7 4.4 slice.205
  344.1 5.6 reshape.599
  349.7 4.4 copy.227
  354.1 5.5 reshape.600
  359.7 5.8 convolution_convert_fusion.2
  368.9 10.3 %all-to-all-start.3 = ((bf16[32,2,256,128]{3,2,1,0:T(8,128)(2,1)}), bf16[32,2,256,128]{3,2,1,0:T(8,128)(2,1)}, u32[]{:S(2)}, u32[]{:S(2)}) async-start(bf16[32,2,256,128]{3,2,1,0:T(8,128)(2,1)} %copy.171), calls=%async_computation.3 | async-start | bytes 8388608 | tf_op jit(solution)/shard_map/all_to_all | solution.py:185
  379.2 4.5 slice.219
  383.6 5.6 reshape.604
  389.3 4.5 copy.226
  393.8 5.3 reshape.605
  399.1 5.8 convolution_convert_fusion.1
  408.2 64.8 %all-to-all-done.3 = bf16[32,2,256,128]{3,2,1,0:T(8,128)(2,1)} async-done(((bf16[32,2,256,128]{3,2,1,0:T(8,128)(2,1)}), bf16[32,2,256,128]{3,2,1,0:T(8,128)(2,1)}, u32[]{:S(2)}, u32[]{:S(2)}) %all-to-all-start.3) | async-done | bytes 4194336 | tf_op jit(solution)/shard_map/all_to_all | solution.py:185
  473.0 8.2 %all-to-all-start.4 = ((bf16[32,2,256,128]{3,2,1,0:T(8,128)(2,1)}), bf16[32,2,256,128]{3,2,1,0:T(8,128)(2,1)}, u32[]{:S(2)}, u32[]{:S(2)}) async-start(bf16[32,2,256,128]{3,2,1,0:T(8,128)(2,1)} %copy.177), calls=%async_computation.4 | async-start | bytes 8388608 | tf_op jit(solution)/shard_map/all_to_all | solution.py:186
  491.0 87.1 %collective-permute-done.2 = bf16[2,2,256,128]{3,2,1,0:T(8,128)(2,1)S(1)} collective-permute-done((bf16[2,2,256,128]{3,2,1,0:T(8,128)(2,1)S(1)}, bf16[2,2,256,128]{3,2,1,0:T(8,128)(2,1)S(1)}, u32[]{:S(2)}, u32[]{:S(2)}) %collective-permute-start.2) | collective-permute-done | bytes 262176 | tf_op jit(solution)/shard_map/ppermute | solution.py:12
  579.8 4.0 collective-permute-done.3
  585.4 5.4 fusion.73
  592.2 4.6 fusion.63
  (118 shorter events, 68.6 us)
Async XLA Ops:
  0.6 12.2 %copy-start.5 = (s32[4,32,2,2]{1,3,2,0:T(2,128)S(1)}, s32[4,32,2,2]{1,3,2,0:T(2,128)}, u32[]{:S(2)}) copy-start(s32[4,32,2,2]{1,3,2,0:T(2,128)} %param.11) | copy-start | bytes 6148
  0.6 12.3 %copy-start.1 = (bf16[4,256,256]{2,1,0:T(8,128)(2,1)S(1)}, bf16[4,256,256]{2,1,0:T(8,128)(2,1)}, u32[]{:S(2)}) copy-start(bf16[4,256,256]{2,1,0:T(8,128)(2,1)} %param.8) | copy-start | bytes 1572868
  6.2 16.0 %all-to-all-start.2 = ((bf16[8,2,16384]{2,1,0:T(2,128)(2,1)}), bf16[8,2,16384]{2,1,0:T(2,128)(2,1)S(1)}, u32[]{:S(2)}, u32[]{:S(2)}) async-start(bf16[8,2,16384]{2,1,0:T(2,128)(2,1)} %reshape.621), calls=%async_computation.2 | async-start | bytes 1048576 | tf_op jit(solution)/shard_map/all_to_all | solution.py:59
  18.4 15.0 %copy-start.2 = (bf16[4,256,256]{2,1,0:T(8,128)(2,1)S(1)}, bf16[4,256,256]{2,1,0:T(8,128)(2,1)}, u32[]{:S(2)}) copy-start(bf16[4,256,256]{2,1,0:T(8,128)(2,1)} %param.9) | copy-start | bytes 1572868
  22.2 0.8 copy-start
  23.0 103.3 %all-to-all-start = ((bf16[32,2,256,128]{3,2,1,0:T(8,128)(2,1)}), bf16[32,2,256,128]{3,2,1,0:T(8,128)(2,1)}, u32[]{:S(2)}, u32[]{:S(2)}) async-start(bf16[32,2,256,128]{3,2,1,0:T(8,128)(2,1)} %copy.144), calls=%async_computation | async-start | bytes 8388608 | tf_op jit(solution)/shard_map/all_to_all | solution.py:90
  126.3 131.0 %all-to-all-start.1 = ((bf16[32,2,256,128]{3,2,1,0:T(8,128)(2,1)}), bf16[32,2,256,128]{3,2,1,0:T(8,128)(2,1)}, u32[]{:S(2)}, u32[]{:S(2)}) async-start(bf16[32,2,256,128]{3,2,1,0:T(8,128)(2,1)} %copy.154), calls=%async_computation.1 | async-start | bytes 8388608 | tf_op jit(solution)/shard_map/all_to_all | solution.py:91
  136.6 102.9 %collective-permute-start = (bf16[2,2,256,128]{2,3,0,1:T(8,128)(2,1)}, bf16[2,2,256,128]{2,3,0,1:T(8,128)(2,1)}, u32[]{:S(2)}, u32[]{:S(2)}) collective-permute-start(bf16[2,2,256,128]{2,3,0,1:T(8,128)(2,1)} %fusion.115), channel_id=1, source_target_pairs={{0,8},{8,0},{16,24},{24,16},{32,40},{40,32},{48,56},{56,48},{64,72... | collective-permute-start | bytes 786440 | tf_op jit(solution)/shard_map/ppermute | solution.py:12
  137.8 100.7 %collective-permute-start.1 = (bf16[2,2,256,128]{2,3,0,1:T(8,128)(2,1)S(1)}, bf16[2,2,256,128]{2,3,0,1:T(8,128)(2,1)S(1)}, u32[]{:S(2)}, u32[]{:S(2)}) collective-permute-start(bf16[2,2,256,128]{2,3,0,1:T(8,128)(2,1)S(1)} %fusion.113), channel_id=1, source_target_pairs={{0,8},{8,0},{16,24},{24,16},{32,40},{40,32},{48,56},{56,48},{64,72... | collective-permute-start | bytes 786440 | tf_op jit(solution)/shard_map/ppermute | solution.py:12
  141.4 7.5 %copy-start.3 = (bf16[4,256,256]{2,1,0:T(8,128)(2,1)S(1)}, bf16[4,256,256]{2,1,0:T(8,128)(2,1)}, u32[]{:S(2)}) copy-start(bf16[4,256,256]{2,1,0:T(8,128)(2,1)} %param.7) | copy-start | bytes 1572868
  368.9 104.1 %all-to-all-start.3 = ((bf16[32,2,256,128]{3,2,1,0:T(8,128)(2,1)}), bf16[32,2,256,128]{3,2,1,0:T(8,128)(2,1)}, u32[]{:S(2)}, u32[]{:S(2)}) async-start(bf16[32,2,256,128]{3,2,1,0:T(8,128)(2,1)} %copy.171), calls=%async_computation.3 | async-start | bytes 8388608 | tf_op jit(solution)/shard_map/all_to_all | solution.py:185
  473.0 119.2 %all-to-all-start.4 = ((bf16[32,2,256,128]{3,2,1,0:T(8,128)(2,1)}), bf16[32,2,256,128]{3,2,1,0:T(8,128)(2,1)}, u32[]{:S(2)}, u32[]{:S(2)}) async-start(bf16[32,2,256,128]{3,2,1,0:T(8,128)(2,1)} %copy.177), calls=%async_computation.4 | async-start | bytes 8388608 | tf_op jit(solution)/shard_map/all_to_all | solution.py:186
  481.2 6.7 %copy-start.4 = (bf16[4,2,256,128]{3,2,1,0:T(8,128)(2,1)S(1)}, bf16[4,2,256,128]{3,2,1,0:T(8,128)(2,1)}, u32[]{:S(2)}) copy-start(bf16[4,2,256,128]{3,2,1,0:T(8,128)(2,1)} %get-tuple-element.59) | copy-start | bytes 1572868
  486.3 91.8 %collective-permute-start.2 = (bf16[2,2,256,128]{3,2,1,0:T(8,128)(2,1)S(1)}, bf16[2,2,256,128]{3,2,1,0:T(8,128)(2,1)S(1)}, u32[]{:S(2)}, u32[]{:S(2)}) collective-permute-start(bf16[2,2,256,128]{3,2,1,0:T(8,128)(2,1)S(1)} %fusion.110), channel_id=1, source_target_pairs={{0,8},{8,0},{16,24},{24,16},{32,40},{40,32},{48,56},{56,48},{64,72... | collective-permute-start | bytes 786440 | tf_op jit(solution)/shard_map/ppermute | solution.py:12
  488.7 95.0 %collective-permute-start.3 = (bf16[2,2,256,128]{3,2,1,0:T(8,128)(2,1)S(1)}, bf16[2,2,256,128]{3,2,1,0:T(8,128)(2,1)S(1)}, u32[]{:S(2)}, u32[]{:S(2)}) collective-permute-start(bf16[2,2,256,128]{3,2,1,0:T(8,128)(2,1)S(1)} %fusion.111), channel_id=1, source_target_pairs={{0,8},{8,0},{16,24},{24,16},{32,40},{40,32},{48,56},{56,48},{64,72... | collective-permute-start | bytes 786440 | tf_op jit(solution)/shard_map/ppermute | solution.py:12
where the time goes:
time: 608 us; the launch traced here: 599 us
  waiting for transfers between devices  335 us (55%)
  matrix products  95.2 us (16%)
  local copies, waits for them, and re-layouts  94.8 us (16%)
  starting transfers between devices  48.8 us (8%)
  other arithmetic  18.1 us (3%)
  between operations  6.46 us (1%)
    ppermute x4, waiting for transfers between devices, from_partner(): lax.ppermute(value, axis, [(i, i ^ 1 << bit) for i in range(lax.axis_size...  179 us
    all_to_all x1, waiting for transfers between devices, local(): lax.all_to_all(send_k, 'seq', split_axis=0, concat_axis=0, tiled=True)  87.5 us
    all_to_all x1, waiting for transfers between devices, local(): lax.all_to_all(outgoing(key_terms), 'seq', split_axis=0, concat_axis=0, t...  64.8 us
    reshape x4, local copies, waits for them, and re-layouts, outgoing(): terms[:, :, block_len:]  20.2 us
    dot_general x4, matrix products, attend(): jnp.einsum('hqk,hqd->hkd', probability_narrow, g_one, preferred_element_t...  17.2 us
    unnamed x22, local copies, waits for them, and re-layouts  15.7 us
    dot_general x4, matrix products, attend(): jnp.einsum('hqk,hkd->hqd', probability_narrow, v_one, preferred_element_t...  15.2 us
  transfers between devices with their start and end apart: 9, of which 6 were waited for; matrix products, arithmetic and copies ran while one was open for 14% of the time, Pallas kernels for 0%

commit v1 on v0

v1 whole, which is shorter than its diff:
```python
import math

import jax
import jax.numpy as jnp
from jax import lax
from jax.sharding import Mesh, PartitionSpec as P

HD = 128


def swap_pair(value):
    return lax.ppermute(value, "sp", [(0, 1), (1, 0)])


def per_head(stored, head_count):
    slices = stored.shape[0]
    rows = stored.shape[1]
    return stored.reshape(slices, rows, head_count, HD).transpose(2, 0, 1, 3)


def merge_heads(split):
    head_count = split.shape[0]
    slices = split.shape[1]
    rows = split.shape[2]
    return split.transpose(1, 2, 0, 3).reshape(slices, rows, head_count * HD)


def local(queries, keys, values, out_grad, selected):
    groups = lax.axis_size("sg")
    seq_count = 2 * groups
    group_id = lax.axis_index("sg")
    parity = lax.axis_index("sp")
    slices = queries.shape[0]
    half_len = queries.shape[1]
    block_len = 2 * half_len
    head_count = queries.shape[2] // HD
    logit_scale_factor = 1.0 / math.sqrt(HD)
    q_heads = per_head(queries, head_count)
    k_heads = per_head(keys, head_count)
    v_heads = per_head(values, head_count)
    grad_rows = lax.all_to_all(out_grad, "head", split_axis=2, concat_axis=1, tiled=True)
    g_heads = per_head(grad_rows, head_count)
    kv = jnp.stack([k_heads, v_heads])

    sel_g = selected[:, 0::2]
    gid = jnp.arange(groups, dtype=jnp.int32)
    query_block = jnp.stack([gid, seq_count - 1 - gid, seq_count + gid, 2 * seq_count - 1 - gid])
    usable_g = sel_g < query_block[:, :, None, None]
    mine_block = jnp.stack(
        [group_id, seq_count - 1 - group_id, seq_count + group_id, 2 * seq_count - 1 - group_id]
    )
    hits = usable_g[..., None] & (sel_g[..., None] == mine_block)
    need = jnp.any(hits, axis=(0, 3)).astype(jnp.bfloat16)
    mine_sel = lax.dynamic_index_in_dim(sel_g, group_id, 1, keepdims=False)
    mine_usable = mine_sel < mine_block[:, None, None]
    fold = mine_sel % seq_count
    src_group = jnp.where(fold >= groups, seq_count - 1 - fold, fold)
    src_group = jnp.where(mine_usable, src_group, 0)

    send = jnp.einsum(
        "ghf,chfld->gchld", need, kv, preferred_element_type=jnp.float32
    ).astype(jnp.bfloat16)
    got = lax.all_to_all(send, "sg", split_axis=0, concat_axis=0, tiled=True)
    got_h = got.transpose(2, 0, 1, 3, 4)
    head_index = jnp.arange(head_count, dtype=jnp.int32)[None, :, None]
    taken = got_h[head_index, src_group]
    held_half = (jnp.arange(slices, dtype=jnp.int32) + parity) % 2
    pairs_kv = kv.reshape(2, head_count, slices // 2, 2, half_len, HD)
    lead = jnp.where(parity == 0, pairs_kv[:, :, :, 0], pairs_kv[:, :, :, 1])
    other, mate = swap_pair((taken, lead))

    empty_span = jnp.zeros((2, head_count, half_len, HD), jnp.bfloat16)
    own_rows = []
    for slice_id in range(slices):
        second = jnp.concatenate([mate[:, :, slice_id // 2], kv[:, :, slice_id]], axis=2)
        first = jnp.concatenate([kv[:, :, slice_id], empty_span], axis=2)
        own_rows.append(jnp.where(held_half[slice_id] == 1, second, first))
    own_kv = jnp.stack(own_rows, axis=0)
    sel_kv = jnp.stack([taken, other], axis=3)
    sel_kv = sel_kv.transpose(0, 4, 1, 2, 3, 5, 6).reshape(
        slices, 2, head_count, 2 * sel_g.shape[3] * half_len, HD
    )
    every_kv = jnp.concatenate([own_kv, sel_kv], axis=3)

    key_pos = jnp.arange(block_len, dtype=jnp.int32)
    query_pos = held_half[:, None] * half_len + jnp.arange(half_len, dtype=jnp.int32)[None, :]
    own_vis = key_pos[None, None, :] <= query_pos[:, :, None]
    sel_vis = jnp.repeat(mine_usable, block_len, axis=2)
    visible = jnp.concatenate(
        [
            jnp.broadcast_to(own_vis[:, None], (slices, head_count, half_len, block_len)),
            jnp.broadcast_to(
                sel_vis[:, :, None, :], (slices, head_count, half_len, sel_vis.shape[2])
            ),
        ],
        axis=-1,
    )

    def attend(operands):
        q_one, k_one, v_one, g_one, vis_one = operands
        attention_logits = (
            jnp.einsum("hqd,hkd->hqk", q_one, k_one, preferred_element_type=jnp.float32)
            * logit_scale_factor
        )
        masked = jnp.where(vis_one, attention_logits, -jnp.inf)
        row_max = jnp.max(masked, axis=-1, keepdims=True)
        exp_vals = jnp.exp(masked - row_max)
        probs = exp_vals / jnp.sum(exp_vals, axis=-1, keepdims=True)
        probability_narrow = probs.astype(jnp.bfloat16)
        attended = jnp.einsum(
            "hqk,hkd->hqd", probability_narrow, v_one, preferred_element_type=jnp.float32
        ).astype(jnp.bfloat16)
        probability_gradient = jnp.einsum(
            "hqd,hkd->hqk", g_one, v_one, preferred_element_type=jnp.float32
        )
        row_delta = jnp.sum(probs * probability_gradient, axis=-1, keepdims=True)
        score_gradient = (probs * (probability_gradient - row_delta)).astype(jnp.bfloat16)
        query_gradient = (
            logit_scale_factor
            * jnp.einsum("hqk,hkd->hqd", score_gradient, k_one, preferred_element_type=jnp.float32)
        ).astype(jnp.bfloat16)
        key_terms = logit_scale_factor * jnp.einsum(
            "hqk,hqd->hkd", score_gradient, q_one, preferred_element_type=jnp.float32
        )
        value_terms = jnp.einsum(
            "hqk,hqd->hkd", probability_narrow, g_one, preferred_element_type=jnp.float32
        )
        return (attended, query_gradient, jnp.stack([key_terms, value_terms]))

    attended, query_gradient, terms = lax.map(
        attend,
        (
            jnp.moveaxis(q_heads, 1, 0),
            every_kv[:, 0],
            every_kv[:, 1],
            jnp.moveaxis(g_heads, 1, 0),
            visible,
        ),
    )

    sel_terms = terms[:, :, :, block_len:].reshape(
        slices, 2, head_count, sel_g.shape[3], 2, half_len, HD
    )
    mine_terms = sel_terms[:, :, :, :, 0]
    other_terms = sel_terms[:, :, :, :, 1].astype(jnp.bfloat16)
    by_pair = terms[:, :, :, :half_len].reshape(slices // 2, 2, 2, head_count, half_len, HD)
    trail = jnp.where(parity == 0, by_pair[:, 1], by_pair[:, 0]).astype(jnp.bfloat16)
    partner_terms, mate_back = swap_pair((other_terms, trail))
    summed = (mine_terms + partner_terms.astype(jnp.float32)).astype(jnp.bfloat16)
    route = (
        (src_group[None] == gid[:, None, None, None]) & mine_usable[None]
    ).astype(jnp.bfloat16)
    send_back = jnp.einsum(
        "gfhj,fchjld->gchld", route, summed, preferred_element_type=jnp.float32
    ).astype(jnp.bfloat16)
    back = lax.all_to_all(send_back, "sg", split_axis=0, concat_axis=0, tiled=True)
    gathered = jnp.einsum("ghf,gchld->chfld", need, back, preferred_element_type=jnp.float32)

    def own_part(kind):
        rows_kept = []
        for slice_id in range(slices):
            first = terms[slice_id, kind, :, :half_len] + mate_back[slice_id // 2, kind].astype(
                jnp.float32
            )
            second = terms[slice_id, kind, :, half_len:block_len]
            rows_kept.append(jnp.where(held_half[slice_id] == 0, first, second))
        return jnp.stack(rows_kept, axis=1)

    key_grad = (own_part(0) + gathered[0]).astype(jnp.bfloat16)
    value_grad = (own_part(1) + gathered[1]).astype(jnp.bfloat16)
    attended_rows = attended.transpose(0, 2, 1, 3).reshape(slices, half_len, head_count * HD)
    query_rows = query_gradient.transpose(0, 2, 1, 3).reshape(slices, half_len, head_count * HD)
    return (attended_rows, query_rows, merge_heads(key_grad), merge_heads(value_grad))


def solution(mesh):
    seq_count = mesh.shape["seq"]
    head_count = mesh.shape["head"]
    pair_mesh = Mesh(
        mesh.devices.reshape(seq_count // 2, 2, head_count), ("sg", "sp", "head")
    )
    tokens = P(None, ("sg", "sp"), "head")
    in_specs = (
        tokens,
        tokens,
        tokens,
        P(None, ("sg", "sp", "head"), None),
        P(None, None, "head", None),
    )
    out_specs = (tokens, tokens, tokens, tokens)
    return jax.shard_map(local, mesh=pair_mesh, in_specs=in_specs, out_specs=out_specs, check_vma=False)
```

time: 608 us -> 461 us (0.76)
  waiting for transfers between devices: 335 us -> 251 us
  local copies, waits for them, and re-layouts: 94.8 us -> 49.3 us
  matrix products: 95.2 us -> 76.9 us
  other arithmetic: 18.1 us -> 33.3 us
  starting transfers between devices: 48.8 us -> 37.1 us
    all_to_all x4 -> x2, waiting for transfers between devices: 152 us -> 79.2 us  [the longest x1 79.2 us: local(): got = lax.all_to_all(send, 'sg', split_axis=0, concat_axis=0, tiled=True)]
    reshape x8 -> x0, local copies, waits for them, and re-layouts: 35.5 us -> none  [the longest x4 20.2 us: outgoing(): terms[:, :, block_len:]]
    all_to_all x4 -> x2, starting transfers between devices: 38.5 us -> 20.3 us  [the longest x1 11.6 us: local(): got = lax.all_to_all(send, 'sg', split_axis=0, concat_axis=0, tiled=True)]
    dot_general x6 -> x3, matrix products: 24.2 us -> 10.1 us  [the longest x1 4.76 us: local(): jnp.einsum('ghf,gchld->chfld', need, back, preferred_element_type=jnp.flo...]
    dynamic_update_slice x0 -> x4, other arithmetic: none -> 7.54 us  [local(): lax.map(attend, (jnp.moveaxis(q_heads, 1, 0), every_kv[:, 0], every_kv[:,...]
    ppermute x4, waiting for transfers between devices: 179 us -> 172 us  [swap_pair(): return lax.ppermute(value, 'sp', [(0, 1), (1, 0)])]
    transpose x3 -> x1, other arithmetic: 9.32 us -> 2.61 us  [local(): sel_kv.transpose(0, 4, 1, 2, 3, 5, 6)]
    all_to_all x1, starting transfers between devices: 6.6 us -> 13.3 us  [local(): lax.all_to_all(out_grad, 'head', split_axis=2, concat_axis=1, tiled=True)]
  transfers between devices with their start and end apart: 9 -> 7, of which waited for: 6 -> 4; matrix products, arithmetic and copies ran while one was open for 14% -> 9% of each run, Pallas kernels for 0% -> 0%
where the time goes in v1:
time: 461 us; the launch traced here: 454 us
  waiting for transfers between devices  251 us (54%)
  matrix products  76.9 us (17%)
  local copies, waits for them, and re-layouts  49.3 us (11%)
  starting transfers between devices  37.1 us (8%)
  other arithmetic  33.3 us (7%)
  between operations  6.18 us (1%)
    ppermute x4, waiting for transfers between devices, swap_pair(): return lax.ppermute(value, 'sp', [(0, 1), (1, 0)])  172 us
    all_to_all x1, waiting for transfers between devices, local(): got = lax.all_to_all(send, 'sg', split_axis=0, concat_axis=0, tiled=True)  79.2 us
    dot_general x4, matrix products, attend(): jnp.einsum('hqk,hqd->hkd', probability_narrow, g_one, preferred_element_t...  17.2 us
    dot_general x4, matrix products, attend(): jnp.einsum('hqk,hkd->hqd', probability_narrow, v_one, preferred_element_t...  15.2 us
    unnamed x21, local copies, waits for them, and re-layouts  13.7 us
    all_to_all x1, starting transfers between devices, local(): lax.all_to_all(out_grad, 'head', split_axis=2, concat_axis=1, tiled=True)  13.3 us
    all_to_all x1, starting transfers between devices, local(): got = lax.all_to_all(send, 'sg', split_axis=0, concat_axis=0, tiled=True)  11.6 us
    sub x4, matrix products, attend(): exp_vals = jnp.exp(masked - row_max)  10.8 us
  transfers between devices with their start and end apart: 7, of which 4 were waited for; matrix products, arithmetic and copies ran while one was open for 9% of the time, Pallas kernels for 0%

profile of v1, /device:TPU:1, one launch (start us, length us, event | category | flops | bytes accessed | tf_op | source)
XLA Modules:
  0.0 454.0 jit_solution(11343322525781827764)
XLA Ops:
  6.9 3.1 copy.264
  10.0 11.6 %all-to-all-start = ((bf16[16,2,2,256,128]{4,3,1,2,0:T(8,128)(2,1)}), bf16[16,2,2,256,128]{4,3,1,2,0:T(8,128)(2,1)}, u32[]{:S(2)}, u32[]{:S(2)}) async-start(bf16[16,2,2,256,128]{4,3,1,2,0:T(8,128)(2,1)} %copy.264), calls=%async_computation | async-start | bytes 8388608 | tf_op jit(solution)/shard_map/all_to_all | solution.py:63
  23.9 2.8 copy.270
  26.8 2.7 reshape.521
  29.9 3.6 fusion.91
  33.5 79.2 %all-to-all-done = bf16[16,2,2,256,128]{4,3,1,2,0:T(8,128)(2,1)} async-done(((bf16[16,2,2,256,128]{4,3,1,2,0:T(8,128)(2,1)}), bf16[16,2,2,256,128]{4,3,1,2,0:T(8,128)(2,1)}, u32[]{:S(2)}, u32[]{:S(2)}) %all-to-all-start) | async-done | bytes 4194336 | tf_op jit(solution)/shard_map/all_to_all | solution.py:63
  112.7 13.3 %all-to-all-start.1 = ((bf16[8,2,16384]{2,1,0:T(2,128)(2,1)}), bf16[8,2,16384]{2,1,0:T(2,128)(2,1)S(1)}, u32[]{:S(2)}, u32[]{:S(2)}) async-start(bf16[8,2,16384]{2,1,0:T(2,128)(2,1)} %reshape.521), calls=%async_computation.1 | async-start | bytes 1048576 | tf_op jit(solution)/shard_map/all_to_all | solution.py:41
  126.0 4.7 %copy.336 = bf16[16,2,2,256,128]{4,3,1,0,2:T(8,128)(2,1)} copy(bf16[16,2,2,256,128]{4,3,1,2,0:T(8,128)(2,1)} %all-to-all-done) | data formatting | bytes 8388608 | tf_op jit(solution)/shard_map/all_to_all | solution.py:63
  130.7 4.3 gather_fusion
  136.6 4.6 %pad_add_fusion = pred[4,2,256,1536]{3,2,1,0:T(32,128)(4,1)} fusion(pred[4,2,256,1024]{3,2,1,0:T(32,128)(4,1)S(1)} %broadcast_in_dim.31, pred[4,2,256,512]{3,2,1,0:T(32,128)(4,1)S(1)} %broadcast_in_dim.28), kind=kLoop, calls=%fused_computation.49 | loop fusion | flops 3145728 | bytes 6291456 | tf_op jit(solution)/shard_map/concatenate | solution.py:89
  151.2 31.3 %collective-permute-done.1 = bf16[4,2,2,2,256,128]{5,4,3,2,1,0:T(8,128)(2,1)} collective-permute-done((bf16[4,2,2,2,256,128]{5,4,3,2,1,0:T(8,128)(2,1)}, bf16[4,2,2,2,256,128]{5,4,3,2,1,0:T(8,128)(2,1)}, u32[]{:S(2)}, u32[]{:S(2)}) %collective-permute-start.1) | collective-permute-done | bytes 2097184 | tf_op jit(solution)/shard_map/ppermute | solution.py:12
  182.5 2.6 maximum_bitcast_fusion.1
  185.6 3.2 fusion.69
  188.8 80.1 %while.14 = (s32[]{:T(128)}, bf16[4,2,256,128]{3,2,1,0:T(8,128)(2,1)}, bf16[4,2,256,128]{3,2,1,0:T(8,128)(2,1)}, f32[4,2,2,1536,128]{4,3,2,1,0:T(8,128)}, pred[4...) while((s32[]{:T(128)}, ...), condition=%wide.region_5.6_spmd, body=%wide.region_1.5_spmd.sunk | while | flops 1628509184 | bytes 48779984 | solution.py:130
  189.7 2.7 fusion.166
  192.4 3.8 fusion.167
  196.2 4.3 convolution_bitcast_fusion.2
  200.5 1.8 multiply_reduce_fusion.2
  202.8 2.5 fusion.168
  207.0 1.9 fusion.170
  209.8 2.7 fusion.166
  212.4 3.8 fusion.167
  216.2 4.3 convolution_bitcast_fusion.2
  220.5 1.8 multiply_reduce_fusion.2
  222.9 2.5 fusion.168
  227.0 1.9 fusion.170
  229.8 2.7 fusion.166
  232.5 3.8 fusion.167
  236.3 4.3 convolution_bitcast_fusion.2
  240.6 1.8 multiply_reduce_fusion.2
  242.9 2.5 fusion.168
  247.0 1.9 fusion.170
  249.9 2.7 fusion.166
  252.5 3.8 fusion.167
  256.3 4.3 convolution_bitcast_fusion.2
  260.6 1.8 multiply_reduce_fusion.2
  263.0 2.5 fusion.168
  267.1 1.9 fusion.170
  269.0 4.0 slice.176
  276.2 45.2 %collective-permute-done.3 = bf16[4,2,2,2,256,128]{5,0,3,4,1,2:T(4,128)(2,1)S(1)} collective-permute-done((bf16[4,2,2,2,256,128]{5,0,3,4,1,2:T(4,128)(2,1)S(1)}, bf16[4,2,2,2,256,128]{5,0,3,4,1,2:T(4,128)(2,1)S(1)}, u32[]{:S(2)}, u32[]{:S(2)}) %collective-permute-start.3) | collective-permute-done | bytes 2097184 | tf_op jit(solution)/shard_map/ppermute | solution.py:12
  321.4 4.1 fusion.62
  325.4 3.0 copy.280
  328.5 8.7 %all-to-all-start.2 = ((bf16[16,2,2,256,128]{4,3,1,2,0:T(8,128)(2,1)}), bf16[16,2,2,256,128]{4,3,1,2,0:T(8,128)(2,1)}, u32[]{:S(2)}, u32[]{:S(2)}) async-start(bf16[16,2,2,256,128]{4,3,1,2,0:T(8,128)(2,1)} %copy.280), calls=%async_computation.2 | async-start | bytes 8388608 | tf_op jit(solution)/shard_map/all_to_all | solution.py:156
  337.2 1.9 slice.164
  344.6 95.4 %collective-permute-done.2 = bf16[2,2,2,256,128]{4,3,2,1,0:T(8,128)(2,1)S(1)} collective-permute-done((bf16[2,2,2,256,128]{4,3,2,1,0:T(8,128)(2,1)S(1)}, bf16[2,2,2,256,128]{4,3,2,1,0:T(8,128)(2,1)S(1)}, u32[]{:S(2)}, u32[]{:S(2)}) %collective-permute-start.2) | collective-permute-done | bytes 524320 | tf_op jit(solution)/shard_map/ppermute | solution.py:12
  441.5 2.8 fusion.105
  444.3 4.8 %fusion.71 = f32[2,2,4,256,128]{4,2,3,0,1:T(4,128)S(1)} fusion(bf16[16,2,2,256,128]{4,3,1,2,0:T(8,128)(2,1)} %all-to-all-done.2, pred[16,2,4]{0,2,1:T(4,128)(4,1)S(1)} %and_reduce_fusion), kind=kOutput, calls=%fused_computation.70 | convolution fusion | flops 16777216 | bytes 6291584 | tf_op jit(solution)/shard_map/ghf,gchld->chfld/dot_general | solution.py:157
  450.5 2.2 fusion.96
  (112 shorter events, 41.0 us)
Async XLA Ops:
  10.0 102.7 %all-to-all-start = ((bf16[16,2,2,256,128]{4,3,1,2,0:T(8,128)(2,1)}), bf16[16,2,2,256,128]{4,3,1,2,0:T(8,128)(2,1)}, u32[]{:S(2)}, u32[]{:S(2)}) async-start(bf16[16,2,2,256,128]{4,3,1,2,0:T(8,128)(2,1)} %copy.264), calls=%async_computation | async-start | bytes 8388608 | tf_op jit(solution)/shard_map/all_to_all | solution.py:63
  22.7 126.0 %collective-permute-start = (bf16[2,2,2,256,128]{4,3,2,1,0:T(8,128)(2,1)}, bf16[2,2,2,256,128]{4,3,2,1,0:T(8,128)(2,1)}, u32[]{:S(2)}, u32[]{:S(2)}) collective-permute-start(bf16[2,2,2,256,128]{4,3,2,1,0:T(8,128)(2,1)} %fusion.89), channel_id=1, source_target_pairs={{0,8},{8,0},{1,9},{9,1},{2,10},{10,2},{3,11},{11,3},{4,12},{12,4},... | collective-permute-start | bytes 1572872 | tf_op jit(solution)/shard_map/ppermute | solution.py:12
  112.7 33.5 %all-to-all-start.1 = ((bf16[8,2,16384]{2,1,0:T(2,128)(2,1)}), bf16[8,2,16384]{2,1,0:T(2,128)(2,1)S(1)}, u32[]{:S(2)}, u32[]{:S(2)}) async-start(bf16[8,2,16384]{2,1,0:T(2,128)(2,1)} %reshape.521), calls=%async_computation.1 | async-start | bytes 1048576 | tf_op jit(solution)/shard_map/all_to_all | solution.py:41
  135.0 47.5 %collective-permute-start.1 = (bf16[4,2,2,2,256,128]{5,4,3,2,1,0:T(8,128)(2,1)}, bf16[4,2,2,2,256,128]{5,4,3,2,1,0:T(8,128)(2,1)}, u32[]{:S(2)}, u32[]{:S(2)}) collective-permute-start(bf16[4,2,2,2,256,128]{5,4,3,2,1,0:T(8,128)(2,1)} %bitcast.47), channel_id=1, source_target_pairs={{0,8},{8,0},{1,9},{9,1},{2,10},{10,2},{3,11},{11,3},{4,12},{12,4},... | collective-permute-start | bytes 6291464 | tf_op jit(solution)/shard_map/ppermute | solution.py:12
  136.6 7.8 %copy-start.6 = (bf16[4,256,256]{2,1,0:T(8,128)(2,1)S(1)}, bf16[4,256,256]{2,1,0:T(8,128)(2,1)}, u32[]{:S(2)}) copy-start(bf16[4,256,256]{2,1,0:T(8,128)(2,1)} %param.7) | copy-start | bytes 1572868
  136.6 8.8 %copy-start.3 = (bf16[2,2,1,256,128]{4,2,3,0,1:T(2,128)(2,1)S(1)}, bf16[2,2,1,256,128]{4,2,3,0,1:T(2,128)(2,1)}, u32[]{:S(2)}) copy-start(bf16[2,2,1,256,128]{4,2,3,0,1:T(2,128)(2,1)} %get-tuple-element.167) | copy-start | bytes 786436
  188.8 0.8 copy-start.1
  202.8 4.1 copy-start
  207.0 1.9 copy-start.2
  208.9 0.8 copy-start.1
  222.8 4.1 copy-start
  227.0 1.9 copy-start.2
  228.9 0.8 copy-start.1
  242.9 4.1 copy-start
  247.0 1.9 copy-start.2
  249.0 0.8 copy-start.1
  262.9 4.1 copy-start
  267.1 1.9 copy-start.2
  274.9 46.4 %collective-permute-start.3 = (bf16[4,2,2,2,256,128]{5,0,3,4,1,2:T(4,128)(2,1)S(1)}, bf16[4,2,2,2,256,128]{5,0,3,4,1,2:T(4,128)(2,1)S(1)}, u32[]{:S(2)}, u32[]{:S(2)}) collective-permute-start(bf16[4,2,2,2,256,128]{5,0,3,4,1,2:T(4,128)(2,1)S(1)} %bitcast.328), channel_id=1, source_target_pairs={{0,8},{8,0},{1,9},{9,1},{2,10},{10,2},{3,11},{11,3},{4,12},{12,4},... | collective-permute-start | bytes 6291464 | tf_op jit(solution)/shard_map/ppermute | solution.py:12
  328.5 115.8 %all-to-all-start.2 = ((bf16[16,2,2,256,128]{4,3,1,2,0:T(8,128)(2,1)}), bf16[16,2,2,256,128]{4,3,1,2,0:T(8,128)(2,1)}, u32[]{:S(2)}, u32[]{:S(2)}) async-start(bf16[16,2,2,256,128]{4,3,1,2,0:T(8,128)(2,1)} %copy.280), calls=%async_computation.2 | async-start | bytes 8388608 | tf_op jit(solution)/shard_map/all_to_all | solution.py:156
  337.2 5.8 %copy-start.8 = (bf16[4,2,256,128]{3,2,1,0:T(8,128)(2,1)S(1)}, bf16[4,2,256,128]{3,2,1,0:T(8,128)(2,1)}, u32[]{:S(2)}) copy-start(bf16[4,2,256,128]{3,2,1,0:T(8,128)(2,1)} %get-tuple-element.53) | copy-start | bytes 1572868
  337.2 6.6 %copy-start.7 = (bf16[4,2,256,128]{3,2,1,0:T(8,128)(2,1)S(1)}, bf16[4,2,256,128]{3,2,1,0:T(8,128)(2,1)}, u32[]{:S(2)}) copy-start(bf16[4,2,256,128]{3,2,1,0:T(8,128)(2,1)} %get-tuple-element.54) | copy-start | bytes 1572868
  339.1 100.9 %collective-permute-start.2 = (bf16[2,2,2,256,128]{4,3,2,1,0:T(8,128)(2,1)S(1)}, bf16[2,2,2,256,128]{4,3,2,1,0:T(8,128)(2,1)S(1)}, u32[]{:S(2)}, u32[]{:S(2)}) collective-permute-start(bf16[2,2,2,256,128]{4,3,2,1,0:T(8,128)(2,1)S(1)} %fusion.90), channel_id=1, source_target_pairs={{0,8},{8,0},{1,9},{9,1},{2,10},{10,2},{3,11},{11,3},{4,12},{12,4},... | collective-permute-start | bytes 1572872 | tf_op jit(solution)/shard_map/ppermute | solution.py:12
  444.3 4.8 %copy-start.4 = (f32[2,1,256,128]{3,2,0,1:T(8,128)S(1)}, f32[2,1,256,128]{3,2,0,1:T(8,128)}, u32[]{:S(2)}) copy-start(f32[2,1,256,128]{3,2,0,1:T(8,128)} %get-tuple-element.157) | copy-start | bytes 786436
  444.3 4.9 %copy-start.5 = (f32[2,1,256,128]{3,2,0,1:T(8,128)S(1)}, f32[2,1,256,128]{3,2,0,1:T(8,128)}, u32[]{:S(2)}) copy-start(f32[2,1,256,128]{3,2,0,1:T(8,128)} %get-tuple-element.159) | copy-start | bytes 786436
